TPU v7x, 32 devices: a whole 2x2x4 slice. The times are simulated.
32 devices in a mesh: dp: 8 (over z, y), tensor: 4 (over x, core).
Axes of the slice: x: 2, y: 2, z: 4, core: 2. Of those that a mesh axis runs over, the one named last changes fastest.
Arguments:
- hidden_in: bfloat16 [32768, 768], P(('dp', 'tensor')), may hold values from -6 to 6
- qkv_weight: bfloat16 [3, 768, 768], P(None, 'tensor'), may hold values from -0.21875 to 0.21875
- qv_bias: bfloat16 [2, 768], P(None, 'tensor'), may hold values from -3 to 3
- out_weight: bfloat16 [768, 768], P('tensor'), may hold values from -1.25 to 1.25
- out_bias: bfloat16 [768], replicated, may hold values from -3 to 3
- norm1_gain: bfloat16 [768], replicated, may hold values from 0.25 to 1.75
- norm1_shift: bfloat16 [768], replicated, may hold values from -3 to 3
- up_weight: bfloat16 [3072, 768], P('tensor'), may hold values from -0.21875 to 0.21875
- up_bias: bfloat16 [3072], P('tensor'), may hold values from -3 to 3
- down_weight: bfloat16 [3072, 768], P('tensor'), may hold values from -0.109375 to 0.109375
- down_bias: bfloat16 [768], replicated, may hold values from -3 to 3
- norm2_gain: bfloat16 [768], replicated, may hold values from 0.25 to 1.75
- norm2_shift: bfloat16 [768], replicated, may hold values from -3 to 3
- out_grad: bfloat16 [32768, 768], P(('dp', 'tensor')), may hold values from -12 to 12
- seq_lengths: int32 [256], P('dp'), may hold values from 32 to 128, as said below
- key_mask: int32 [32768], P('dp'), may hold values 0 or 1
- split_pos: int32 [256], P('dp'), may hold values from 8 to 95, as said below
Outputs:
- layer_out: bfloat16 [32768, 768], P(('dp', 'tensor'))
- input_grad: bfloat16 [32768, 768], P(('dp', 'tensor'))
- grad_qkv_weight: float32 [3, 768, 768], P(None, 'tensor')
- grad_qv_bias: float32 [2, 768], P(None, 'tensor')
- grad_out_weight: float32 [768, 768], P('tensor')
- grad_out_bias: float32 [768], replicated
- grad_norm1_gain: float32 [768], replicated
- grad_norm1_shift: float32 [768], replicated
- grad_up_weight: float32 [3072, 768], P('tensor')
- grad_up_bias: float32 [3072], P('tensor')
- grad_down_weight: float32 [3072, 768], P('tensor')
- grad_down_bias: float32 [768], replicated
- grad_norm2_gain: float32 [768], replicated
- grad_norm2_shift: float32 [768], replicated
Inputs may be any that keep to these rules, and one draw needn't show every extreme that they name: `seq_lengths`: every slot's length is at least a quarter of 128; the first slot of each index of dp is full. `split_pos`: a slot's split position is at least its length // 4 (a quarter, rounded down) and below three quarters of it.
All inputs are finite; a program needn't handle non-finite values. No bound on the sum of `key_mask` on one device may be relied on, other than what follows from the above.
Results may differ from a plain program's by a relative error of at most 0.019.
Values may be sent and summed in bfloat16 or wider, within the bound.
No kernel may reach another device: no remote copies, remote signals or barrier semaphores. Data moves between devices by JAX's collectives and lax.ppermute only.
A program may use at most 192 MiB of HBM per device.

v0:
```python
import jax
import jax.numpy as jnp
from jax import lax
from jax.sharding import PartitionSpec as P

HD = 64
EPSILON = 1e-05
ROOT_HALF = 0.7071067811865476
DENSITY = 0.3989422804014327
F32 = jnp.float32
BF16 = jnp.bfloat16


def norm_forward(hidden, norm_gain, norm_offset):
    average = jnp.mean(hidden, axis=1, keepdims=True)
    centred = hidden - average
    spread = jnp.mean(centred * centred, axis=1, keepdims=True)
    inverse = lax.rsqrt(spread + EPSILON)
    normal = centred * inverse
    return (normal * norm_gain + norm_offset, normal, inverse)


def norm_backward(upstream, normal, inverse, norm_gain):
    scaled = upstream * norm_gain
    first_mean = jnp.mean(scaled, axis=1, keepdims=True)
    second_mean = jnp.mean(scaled * normal, axis=1, keepdims=True)
    return inverse * (scaled - first_mean - normal * second_mean)


def gelu_parts(before):
    cumulative = 0.5 * (1.0 + jax.scipy.special.erf(before * ROOT_HALF))
    density = DENSITY * jnp.exp(-0.5 * before * before)
    return (before * cumulative, cumulative + before * density)


def body(
    hidden_in,
    qkv_weight,
    qv_bias,
    out_weight,
    out_bias,
    norm1_gain,
    norm1_shift,
    up_weight,
    up_bias,
    down_weight,
    down_bias,
    norm2_gain,
    norm2_shift,
    out_grad,
    seq_lengths,
    key_mask,
    split_pos,
):
    rows = hidden_in.shape[0]
    part_count = lax.axis_size("tensor")
    part_index = lax.axis_index("tensor")
    group_slots = seq_lengths.shape[0]
    slot_len = rows * part_count // group_slots
    slots = rows // slot_len
    width = hidden_in.shape[1]
    heads = width // HD
    w_qkv = lax.all_gather(qkv_weight, "tensor", axis=1, tiled=True)
    b_qv = lax.all_gather(qv_bias, "tensor", axis=1, tiled=True)
    w_out = lax.all_gather(out_weight, "tensor", axis=0, tiled=True)
    w_up = lax.all_gather(up_weight, "tensor", axis=0, tiled=True)
    b_up = lax.all_gather(up_bias, "tensor", axis=0, tiled=True)
    w_down = lax.all_gather(down_weight, "tensor", axis=0, tiled=True)
    lengths = lax.dynamic_slice_in_dim(seq_lengths, part_index * slots, slots)
    splits = lax.dynamic_slice_in_dim(split_pos, part_index * slots, slots)
    mask = lax.dynamic_slice_in_dim(key_mask, part_index * rows, rows).reshape(slots, slot_len)
    places = lax.broadcasted_iota(jnp.int32, (slots, slot_len), 1)
    valid = (places < lengths[:, None]) & ((mask == 1) | (places == 0))
    target = (
        ((places >= splits[:, None]) & (places < lengths[:, None])).astype(F32).reshape(rows, 1)
    )
    gain_mid = norm1_gain.astype(F32)
    shift_mid = norm1_shift.astype(F32)
    gain_out = norm2_gain.astype(F32)
    shift_out = norm2_shift.astype(F32)
    projected = jnp.einsum("rd,cld->crl", hidden_in, w_qkv, preferred_element_type=F32)
    bias_rows = jnp.stack([b_qv[0], jnp.zeros_like(b_qv[0]), b_qv[1]]).astype(F32)
    projected = (projected + bias_rows[:, None, :]).astype(BF16)
    head_shape = (slots, slot_len, heads, HD)
    queries = projected[0].reshape(head_shape)
    key_rows = projected[1].reshape(head_shape)
    value_rows = projected[2].reshape(head_shape)
    scores = jnp.einsum("sqhe,skhe->shqk", queries, key_rows, preferred_element_type=F32) * HD ** (
        -0.5
    )
    masked = jnp.where(valid[:, None, None, :], scores, -1e30)
    largest = jnp.max(masked, axis=-1, keepdims=True)
    weights_raw = jnp.exp(masked - largest)
    totals = jnp.sum(weights_raw, axis=-1, keepdims=True)
    probability = weights_raw / totals
    prob_low = probability.astype(BF16)
    context = jnp.einsum("shqk,skhe->sqhe", prob_low, value_rows, preferred_element_type=F32)
    context_rows = context.astype(BF16).reshape(rows, width)
    attn_out = jnp.dot(context_rows, w_out, preferred_element_type=F32)
    first_sum = hidden_in.astype(F32) + attn_out + out_bias.astype(F32)
    mid_rows, mid_normal, mid_inverse = norm_forward(first_sum, gain_mid, shift_mid)
    mid_low = mid_rows.astype(BF16)
    before = jnp.einsum("rd,fd->rf", mid_low, w_up, preferred_element_type=F32) + b_up.astype(F32)
    activated, gelu_slope = gelu_parts(before)
    activated_low = activated.astype(BF16)
    ffn_out = jnp.dot(activated_low, w_down, preferred_element_type=F32)
    second_sum = mid_rows + ffn_out + down_bias.astype(F32)
    out_rows, out_normal, out_inverse = norm_forward(second_sum, gain_out, shift_out)
    layer_out = out_rows.astype(BF16)
    upstream = out_grad.astype(F32) * target
    grad_gain_out = jnp.sum(upstream * out_normal, axis=0)
    grad_shift_out = jnp.sum(upstream, axis=0)
    second_grad = norm_backward(upstream, out_normal, out_inverse, gain_out)
    grad_down_bias = jnp.sum(second_grad, axis=0)
    second_low = second_grad.astype(BF16)
    grad_down = jnp.einsum("rf,rd->fd", activated_low, second_low, preferred_element_type=F32)
    grad_down = lax.psum(
        lax.psum_scatter(grad_down, "tensor", scatter_dimension=0, tiled=True), "dp"
    )
    activated_grad = jnp.einsum("rd,fd->rf", second_low, w_down, preferred_element_type=F32)
    before_low = (activated_grad * gelu_slope).astype(BF16)
    grad_up = jnp.einsum("rf,rd->fd", before_low, mid_low, preferred_element_type=F32)
    grad_up_bias = jnp.sum(before_low, axis=0, dtype=F32)
    grad_up = lax.psum(lax.psum_scatter(grad_up, "tensor", scatter_dimension=0, tiled=True), "dp")
    grad_up_bias = lax.psum(
        lax.psum_scatter(grad_up_bias, "tensor", scatter_dimension=0, tiled=True), "dp"
    )
    mid_grad = second_grad + jnp.dot(before_low, w_up, preferred_element_type=F32)
    grad_gain_mid = jnp.sum(mid_grad * mid_normal, axis=0)
    grad_shift_mid = jnp.sum(mid_grad, axis=0)
    first_grad = norm_backward(mid_grad, mid_normal, mid_inverse, gain_mid)
    grad_out_bias = jnp.sum(first_grad, axis=0)
    first_low = first_grad.astype(BF16)
    grad_out_weight = jnp.einsum("rl,rd->ld", context_rows, first_low, preferred_element_type=F32)
    grad_out_weight = lax.psum(
        lax.psum_scatter(grad_out_weight, "tensor", scatter_dimension=0, tiled=True), "dp"
    )
    context_grad = (
        jnp.einsum("rd,ld->rl", first_low, w_out, preferred_element_type=F32)
        .astype(BF16)
        .reshape(head_shape)
    )
    prob_grad = jnp.einsum("sqhe,skhe->shqk", context_grad, value_rows, preferred_element_type=F32)
    inner_sum = jnp.sum(probability * prob_grad, axis=-1, keepdims=True)
    score_grad = (probability * (prob_grad - inner_sum)).astype(BF16)
    query_grad = jnp.einsum(
        "shqk,skhe->sqhe", score_grad, key_rows, preferred_element_type=F32
    ) * HD ** (-0.5)
    key_grad = jnp.einsum(
        "shqk,sqhe->skhe", score_grad, queries, preferred_element_type=F32
    ) * HD ** (-0.5)
    value_grad = jnp.einsum("shqk,sqhe->skhe", prob_low, context_grad, preferred_element_type=F32)
    projected_grad = jnp.stack(
        [
            query_grad.reshape(rows, width),
            key_grad.reshape(rows, width),
            value_grad.reshape(rows, width),
        ]
    ).astype(BF16)
    grad_qkv = jnp.einsum("crl,rd->cld", projected_grad, hidden_in, preferred_element_type=F32)
    bias_sums = jnp.sum(projected_grad, axis=1, dtype=F32)
    grad_qv_bias = jnp.stack([bias_sums[0], bias_sums[2]])
    input_grad = (
        first_grad + jnp.einsum("crl,cld->rd", projected_grad, w_qkv, preferred_element_type=F32)
    ).astype(BF16)
    grad_qkv = lax.psum(lax.psum_scatter(grad_qkv, "tensor", scatter_dimension=1, tiled=True), "dp")
    grad_qv_bias = lax.psum(
        lax.psum_scatter(grad_qv_bias, "tensor", scatter_dimension=1, tiled=True), "dp"
    )
    grad_out_bias, grad_gain_mid, grad_shift_mid, grad_down_bias, grad_gain_out, grad_shift_out = (
        lax.psum(
            (
                grad_out_bias,
                grad_gain_mid,
                grad_shift_mid,
                grad_down_bias,
                grad_gain_out,
                grad_shift_out,
            ),
            ("dp", "tensor"),
        )
    )
    return (
        layer_out,
        input_grad,
        grad_qkv,
        grad_qv_bias,
        grad_out_weight,
        grad_out_bias,
        grad_gain_mid,
        grad_shift_mid,
        grad_up,
        grad_up_bias,
        grad_down,
        grad_down_bias,
        grad_gain_out,
        grad_shift_out,
    )


def solution(mesh):
    in_specs = (
        P(("dp", "tensor"), None),
        P(None, "tensor", None),
        P(None, "tensor"),
        P("tensor", None),
        P(),
        P(),
        P(),
        P("tensor", None),
        P("tensor"),
        P("tensor", None),
        P(),
        P(),
        P(),
        P(("dp", "tensor"), None),
        P("dp"),
        P("dp"),
        P("dp"),
    )
    out_specs = (
        P(("dp", "tensor"), None),
        P(("dp", "tensor"), None),
        P(None, "tensor", None),
        P(None, "tensor"),
        P("tensor", None),
        P(),
        P(),
        P(),
        P("tensor", None),
        P("tensor"),
        P("tensor", None),
        P(),
        P(),
        P(),
    )
    return jax.shard_map(body, mesh=mesh, in_specs=in_specs, out_specs=out_specs, check_vma=False)
```

profile of v0, /device:TPU:0, one launch (start us, length us, event | category | flops | bytes accessed | tf_op | source)
XLA Modules:
  0.0 752.3 jit_solution(9560384906454295733)
XLA Ops:
  10.3 6.0 all-gather
  16.4 0.8 convert_bitcast_fusion
  17.2 1.6 copy.80
  18.9 5.5 all-gather.1
  24.4 1.6 copy.88
  26.2 16.9 %all-gather.7.cloned.1.call-done = bf16[3,768,768]{2,1,0:T(8,128)(2,1)} async-done(((bf16[3,192,768]{2,1,0:T(8,128)(2,1)}), bf16[3,768,768]{2,1,0:T(8,128)(2,1)}) %all-gather.7.cloned.1.call-update) | async-done | bytes 3538960 | tf_op jit(solution)/shard_map/all_gather | solution.py:63
  43.2 6.1 fusion.8
  49.3 1.1 slice_bitcast_fusion.1
  52.0 1.1 fusion.41
  53.0 2.7 fusion.64
  55.7 1.0 fusion.27
  56.7 1.6 copy-done.7
  58.3 2.4 copy.86
  60.7 1.5 all-gather.9.cloned.1.call-done
  62.2 3.8 fusion.65
  66.4 34.8 %all-gather.11.cloned.1.call-done = bf16[3072,768]{1,0:T(8,128)(2,1)} async-done(((bf16[768,768]{1,0:T(8,128)(2,1)}), bf16[3072,768]{1,0:T(8,128)(2,1)}) %all-gather.11.cloned.1.call-update) | async-done | bytes 4718608 | tf_op jit(solution)/shard_map/all_gather | solution.py:66
  101.2 12.8 %multiply_convert_fusion = (bf16[1024,3072]{1,0:T(8,128)(2,1)}, f32[1024,3072]{1,0:T(8,128)}) fusion(f32[3072]{0:T(1024)S(1)} %bitcast.117, bf16[3072,768]{1,0:T(8,128)(2,1)} %all-gather.11.cloned.1.call-done, f32[1024,768]{0,1:T(8,128)S(1)} %get-tuple-element.92, f32[768]{0:T(1024)S(1)} %convert_element_type.102, f32[768]{0:T(1024)S(1)} %convert_element_type.101, ...), kind=kOutput, calls=%fused_computation.9 | convolution fusion | flops 4854644736 | bytes 26765312 | tf_op jit(solution)/shard_map/rd,fd->rf/dot_general | solution.py:103
  114.1 26.0 %all-gather.13.cloned.1.call-done = bf16[3072,768]{1,0:T(8,128)(2,1)} async-done(((bf16[768,768]{1,0:T(8,128)(2,1)}), bf16[3072,768]{1,0:T(8,128)(2,1)}) %all-gather.13.cloned.1.call-update) | async-done | bytes 4718608 | tf_op jit(solution)/shard_map/all_gather | solution.py:68
  140.1 9.4 %fusion.66 = (f32[1024]{0:T(1024)S(1)}, f32[1024,768]{0,1:T(8,128)S(1)}) fusion(f32[768]{0:T(1024)S(1)} %convert_element_type.106, bf16[1024,3072]{1,0:T(8,128)(2,1)} %get-tuple-element.93, bf16[3072,768]{1,0:T(8,128)(2,1)} %all-gather.13.cloned.1.call-done, f32[768]{0:T(1024)S(1)} %convert_element_type.102, f32[768]{0:T(1024)S(1)} %convert_element_type.101, ...), kind=kOutput, calls=%fused_computation.113 | convolution fusion | flops 4837342208 | bytes 17323008 | tf_op jit(solution)/shard_map/dot_general | solution.py:106
  149.9 1.0 copy-done.4
  150.9 0.9 fusion.12
  152.4 12.6 %convert_reduce_fusion = (f32[3072]{0:T(1024)S(1)}, bf16[1024,3072]{1,0:T(8,128)(2,1)}) fusion(f32[1024,3072]{1,0:T(8,128)} %get-tuple-element.94, f32[3072]{0:T(1024)S(1)} %bitcast.118, bf16[3072,768]{1,0:T(8,128)(2,1)S(1)} %copy-done.26, f32[1024]{0:T(1024)S(1)} %get-tuple-element.102, f32[1024,768]{0,1:T(8,128)S(1)} %get-tuple-element.96, ...), kind=kOutput, calls=%fused_computation.8 | convolution fusion | flops 4880593920 | bytes 28359680 | tf_op jit(solution)/shard_map/rd,fd->rf/dot_general | solution.py:120
  165.0 11.2 %multiply_reduce_fusion.2 = (f32[768]{0:T(1024)S(1)}, f32[1024]{0:T(1024)S(1)}, f32[1024]{0:T(1024)S(1)}, f32[768]{0:T(1024)S(1)}, f32[1024,768]{0,1:T(8,128)S(1)}) fusion(f32[1024,768]{0,1:T(8,128)S(1)} %copy-done.6, f32[1024]{0:T(1024)S(1)} %add_rsqrt_fusion.1, f32[1024]{0:T(1024)S(1)} %broadcast_multiply_fusion.5, f32[768]{0:T(1024)S(1)} %convert_element_type.101, ...), kind=kOutput, calls=%fused_computation.23 | convolution fusion | flops 4846776320 | bytes 22069248 | tf_op jit(solution)/shard_map/dot_general | solution.py:128
  176.3 1.1 fusion.61
  177.4 1.6 copy-done.8
  179.0 2.8 fusion.17
  181.9 4.8 convolution_convert_fusion.1
  186.8 2.8 copy.90
  189.5 2.1 copy.124
  191.7 7.5 multiply_reduce_fusion
  199.2 5.0 multiply_convert_fusion.1
  204.2 1.0 fusion.25
  205.9 2.4 copy.95
  208.3 3.7 stack_reshape.12
  212.0 2.6 copy.102
  214.6 4.6 fusion.26
  219.2 2.4 copy.98
  221.6 3.7 stack_reshape.13
  225.3 2.8 copy.103
  228.1 5.5 fusion.30
  233.6 2.4 copy.101
  236.1 3.7 stack_reshape.14
  239.7 2.6 copy.104
  242.3 9.7 %fusion.20 = f32[3,768,768]{2,1,0:T(8,128)} fusion(bf16[1024,768]{1,0:T(8,128)(2,1)} %param.17, bf16[1,1024,768]{2,1,0:T(8,128)(2,1)} %copy.104, bf16[1,1024,768]{2,1,0:T(8,128)(2,1)} %copy.103, bf16[1,1024,768]{2,1,0:T(8,128)(2,1)} %copy.102), kind=kOutput, calls=%fused_computation.58 | convolution fusion | flops 3628597248 | bytes 13369344 | tf_op jit(solution)/shard_map/crl,rd->cld/dot_general | solution.py:160
  252.1 11.7 %fusion.47 = f32[3072,768]{1,0:T(8,128)} fusion(bf16[1024,3072]{1,0:T(8,128)(2,1)} %get-tuple-element.93, bf16[1024,768]{0,1:T(8,128)(2,1)} %copy.88, f32[1024,768]{0,1:T(8,128)S(1)} %get-tuple-element.96, f32[1024]{0:T(1024)S(1)} %get-tuple-element.102, f32[1024]{0:T(1024)S(1)} %get-tuple-element.103, f32[1024]{0:T(1024)S(1)} %get-tuple-element.87, ...), kind=kOutput, calls=%fused_computation.81 | convolution fusion | flops 4839702528 | bytes 20470784 | tf_op jit(solution)/shard_map/rf,rd->fd/dot_general | solution.py:116
  263.9 11.9 %fusion.56 = f32[3072,768]{1,0:T(8,128)} fusion(bf16[1024,3072]{1,0:T(8,128)(2,1)} %get-tuple-element.101, f32[1024,768]{0,1:T(8,128)} %copy-done.5, f32[768]{0:T(1024)S(1)} %convert_element_type.102, f32[768]{0:T(1024)S(1)} %convert_element_type.101, f32[1024]{0:T(1024)S(1)} %add_rsqrt_fusion.1, f32[1024]{0:T(1024)S(1)} %broadcast_multiply_fusion.5), kind=kOutput, calls=%fused_computation.105 | convolution fusion | flops 4835770368 | bytes 18888704 | tf_op jit(solution)/shard_map/rf,rd->fd/dot_general | solution.py:122
  275.9 2.7 convert_reduce_fusion.1
  278.6 0.9 copy.118
  279.6 36.0 %reduce-scatter.8.cloned.1.call-done = f32[3,192,768]{2,1,0:T(8,128)} async-done(((f32[3,768,768]{2,1,0:T(8,128)}), f32[3,192,768]{2,1,0:T(8,128)}) %reduce-scatter.8.cloned.1.call-update) | async-done | bytes 1769488 | tf_op jit(solution)/shard_map/reduce_scatter | solution.py:166
  315.7 80.5 %reduce-scatter.14.cloned.1.call-done = f32[768,768]{1,0:T(8,128)} async-done(((f32[3072,768]{1,0:T(8,128)}), f32[768,768]{1,0:T(8,128)}) %reduce-scatter.14.cloned.1.call-update) | async-done | bytes 2359312 | tf_op jit(solution)/shard_map/reduce_scatter | solution.py:118
  396.2 80.6 %reduce-scatter.12.cloned.1.call-done = f32[768,768]{1,0:T(8,128)} async-done(((f32[3072,768]{1,0:T(8,128)}), f32[768,768]{1,0:T(8,128)}) %reduce-scatter.12.cloned.1.call-update) | async-done | bytes 2359312 | tf_op jit(solution)/shard_map/reduce_scatter | solution.py:124
  478.7 9.3 %fusion.9 = bf16[1024,768]{0,1:T(8,128)(2,1)} fusion(f32[1024,768]{0,1:T(8,128)} %copy-done.8, bf16[3,768,768]{2,1,0:T(8,128)(2,1)} %all-gather.7.cloned.1.call-done, bf16[1,1024,768]{2,1,0:T(8,128)(2,1)} %copy.104, bf16[1,1024,768]{2,1,0:T(8,128)(2,1)} %copy.103, bf16[1,1024,768]{2,1,0:T(8,128)(2,1)} %copy.102), kind=kOutput, calls=%fused_computation.21 | convolution fusion | flops 3630170112 | bytes 12976128 | tf_op jit(solution)/shard_map/crl,cld->rd/dot_general | solution.py:164
  488.0 2.6 copy.108
  490.6 4.2 multiply_reduce_fusion.1
  494.9 2.6 copy.107
  497.5 10.1 %all-reduce = f32[3072]{0:T(1024)S(1)} all-reduce(f32[3072]{0:T(1024)S(1)} %get-tuple-element.100), channel_id=6, replica_groups=mesh['dp'=8,'tensor'=4] {'tensor'}, use_global_device_ids=true, to_apply=%region_27.28.clone | all-reduce | flops 3072 | bytes 24576
  507.6 45.4 %all-reduce.1 = (f32[768]{0:T(1024)}, f32[768]{0:T(1024)}, f32[768]{0:T(1024)}, f32[768]{0:T(1024)}, f32[768]{0:T(1024)}, /*index=5*/f32[768]{0:T(1024)}) all-reduce(f32[768]{0:T(1024)S(1)} %get-tuple-element.77, f32[768]{0:T(1024)S(1)} %get-tuple-element.56, ...), channel_id=1, replica_groups=mesh['dp'=8,'tensor'=4] {'dp','tensor'}, use_global_device_ids=true, to_apply=%region_19.20 | all-reduce | flops 4608 | bytes 36864 | tf_op jit(solution)/shard_map/psum | solution.py:171
  553.0 1.0 copy.119
  554.0 23.0 %all-reduce.2 = (f32[2,192]{1,0:T(2,128)}, f32[768]{0:T(1024)}) all-reduce(f32[2,192]{1,0:T(2,128)S(1)} %copy.119, f32[768]{0:T(1024)S(1)} %dynamic-slice.1), channel_id=1, replica_groups=mesh['dp'=8,'tensor'=4] {'dp'}, use_global_device_ids=true, to_apply=%region_15.16 | all-reduce | flops 1152 | bytes 9216 | tf_op jit(solution)/shard_map/psum | solution.py:167
  577.0 161.4 %all-reduce.6.cloned.1.call-done = (f32[3,192,768]{2,1,0:T(8,128)}, f32[192,768]{1,0:T(8,128)}, f32[768,768]{1,0:T(8,128)}, f32[768,768]{1,0:T(8,128)}) async-done(((f32[3,192,768]{2,1,0:T(8,128)}, f32[192,768]{1,0:T(8,128)}, f32[768,768]{1,0:T(8,128)}, f32[768,768]{1,0:T(8,128)}), (f32[3,192,768]{2,1,0:T(8,128)}, f32[192,768]{1,0:T(8,128)}, f32[768,768]{1,0:T(8,128)}, ...) | async-done | bytes 7077904 | tf_op jit(solution)/shard_map/psum | solution.py:166
  738.4 2.9 copy.159
  741.4 0.8 copy.160
  742.2 1.4 copy.161
  743.6 1.4 copy.162
  (116 shorter events, 8.7 us)
Async XLA Ops:
  7.2 3.0 copy-start.27
  7.2 3.0 copy-start.28
  7.2 3.1 copy-start.25
  7.2 10.0 %copy-start.12 = (bf16[1024,768]{1,0:T(8,128)(2,1)S(1)}, bf16[1024,768]{1,0:T(8,128)(2,1)}, u32[]{:S(2)}) copy-start(bf16[1024,768]{1,0:T(8,128)(2,1)} %param.17) | copy-start | bytes 4718596
  7.2 35.9 %all-gather.7.cloned.1.call-start = ((), (), s32[]{:S(2)}) async-start(), calls=%async_computation.5 | async-start | bytes 4423680 | tf_op jit(solution)/shard_map/all_gather | solution.py:63
  8.0 10.9 %copy-start.18 = (bf16[768]{0:T(1024)(128)(2,1)S(1)}, bf16[768]{0:T(1024)(128)(2,1)}, u32[]{:S(2)}) copy-start(bf16[768]{0:T(1024)(128)(2,1)} %param.21) | copy-start | bytes 4612
  8.0 10.9 %copy-start.19 = (bf16[768]{0:T(1024)(128)(2,1)S(1)}, bf16[768]{0:T(1024)(128)(2,1)}, u32[]{:S(2)}) copy-start(bf16[768]{0:T(1024)(128)(2,1)} %param.22) | copy-start | bytes 4612
  8.0 10.9 %copy-start.20 = (bf16[768]{0:T(1024)(128)(2,1)S(1)}, bf16[768]{0:T(1024)(128)(2,1)}, u32[]{:S(2)}) copy-start(bf16[768]{0:T(1024)(128)(2,1)} %param.23) | copy-start | bytes 4612
  8.0 10.9 %copy-start.24 = (bf16[768]{0:T(1024)(128)(2,1)S(1)}, bf16[768]{0:T(1024)(128)(2,1)}, u32[]{:S(2)}) copy-start(bf16[768]{0:T(1024)(128)(2,1)} %param.25) | copy-start | bytes 4612
  8.0 16.4 %copy-start.21 = (bf16[768]{0:T(1024)(128)(2,1)S(1)}, bf16[768]{0:T(1024)(128)(2,1)}, u32[]{:S(2)}) copy-start(bf16[768]{0:T(1024)(128)(2,1)} %param.27) | copy-start | bytes 4612
  8.0 16.4 %copy-start.11 = (bf16[1024,768]{1,0:T(8,128)(2,1)S(1)}, bf16[1024,768]{1,0:T(8,128)(2,1)}, u32[]{:S(2)}) copy-start(bf16[1024,768]{1,0:T(8,128)(2,1)} %param.30) | copy-start | bytes 4718596
  8.0 54.2 %all-gather.9.cloned.1.call-start = ((), (), s32[]{:S(2)}) async-start(), calls=%async_computation.6 | async-start | bytes 1474560 | tf_op jit(solution)/shard_map/all_gather | solution.py:65
  8.8 92.4 %all-gather.11.cloned.1.call-start = ((), (), s32[]{:S(2)}) async-start(), calls=%async_computation.7 | async-start | bytes 5898240 | tf_op jit(solution)/shard_map/all_gather | solution.py:66
  9.5 130.6 %all-gather.13.cloned.1.call-start = ((), (), s32[]{:S(2)}) async-start(), calls=%async_computation.8 | async-start | bytes 5898240 | tf_op jit(solution)/shard_map/all_gather | solution.py:68
  10.1 269.6 %reduce-scatter.10.cloned.1.call-start = ((), (), s32[]{:S(2)}) async-start(), calls=%async_computation.10 | async-start | bytes 2949120 | tf_op jit(solution)/shard_map/reduce_scatter | solution.py:136
  17.2 8.9 %copy-start.22 = (bf16[768]{0:T(1024)(128)(2,1)S(1)}, bf16[768]{0:T(1024)(128)(2,1)}, u32[]{:S(2)}) copy-start(bf16[768]{0:T(1024)(128)(2,1)} %param.28) | copy-start | bytes 4612
  50.8 1.2 copy-start.1
  51.3 1.8 copy-start.2
  51.7 4.0 copy-start.13
  55.7 2.6 copy-start.7
  66.0 48.0 %copy-start.5 = (f32[1024,768]{0,1:T(8,128)}, f32[1024,768]{0,1:T(8,128)S(1)}, u32[]{:S(2)}) copy-start(f32[1024,768]{0,1:T(8,128)S(1)} %get-tuple-element.92) | copy-start | bytes 9437188
  149.5 1.4 copy-start.4
  149.9 2.5 copy-start.26
  152.4 12.6 %copy-start.6 = (f32[1024,768]{0,1:T(8,128)S(1)}, f32[1024,768]{0,1:T(8,128)}, u32[]{:S(2)}) copy-start(f32[1024,768]{0,1:T(8,128)} %copy-done.5) | copy-start | bytes 9437188
  176.2 2.8 copy-start.15
  177.4 1.6 copy-start.8
  181.9 133.8 %reduce-scatter.8.cloned.1.call-start = ((), (), s32[]{:S(2)}) async-start(), calls=%async_computation.9 | async-start | bytes 8847360 | tf_op jit(solution)/shard_map/reduce_scatter | solution.py:166
  189.5 2.1 copy-start.14
  191.6 7.6 %copy-start.16 = (bf16[96,8,8,128]{3,2,1,0:T(8,128)(2,1)}, bf16[96,8,8,128]{3,2,1,0:T(8,128)(2,1)S(1)}, u32[]{:S(2)}) copy-start(bf16[96,8,8,128]{3,2,1,0:T(8,128)(2,1)S(1)} %copy.124) | copy-start | bytes 4718596
  191.7 7.6 %slice-start = ((s8[6291456]{0:T(1024)(128)(4,1)}), s8[4194304]{0:T(1024)(128)(4,1)S(1)}, s32[]{:S(2)}) async-start(s8[6291456]{0:T(1024)(128)(4,1)} %bitcast.106), calls=%async_computation.15 | async-start | bytes 8388608
  191.7 7.5 %slice-start.1 = ((s8[6291456]{0:T(1024)(128)(4,1)}), s8[2097152]{0:T(1024)(128)(4,1)S(1)}, s32[]{:S(2)}) async-start(s8[6291456]{0:T(1024)(128)(4,1)} %bitcast.106), calls=%async_computation.16 | async-start | bytes 4194304
  199.2 5.0 copy-start.3
  204.2 1.7 copy-start
  252.0 144.2 %reduce-scatter.14.cloned.1.call-start = ((), (), s32[]{:S(2)}) async-start(), calls=%async_computation.12 | async-start | bytes 11796480 | tf_op jit(solution)/shard_map/reduce_scatter | solution.py:118
  263.8 212.9 %reduce-scatter.12.cloned.1.call-start = ((), (), s32[]{:S(2)}) async-start(), calls=%async_computation.11 | async-start | bytes 11796480 | tf_op jit(solution)/shard_map/reduce_scatter | solution.py:124
  275.8 277.2 %reduce-scatter.16.cloned.1.call-start = ((), (), s32[]{:S(2)}) async-start(), calls=%async_computation.13 | async-start | bytes 491520
  279.6 458.8 %all-reduce.6.cloned.1.call-start = ((), (), s32[]{:S(2)}) async-start(), calls=%async_computation.14 | async-start | bytes 14155776 | tf_op jit(solution)/shard_map/psum | solution.py:166
  476.8 0.7 copy-start.23
  476.8 0.7 copy-start.29
  738.4 3.0 copy-start.17
  738.4 3.8 copy-start.10
  741.4 2.2 copy-start.9
Sparse Core Ops, SparseCore 0:
  9.6 33.5 all-gather.6
  44.7 17.4 all-gather.8
  63.7 37.4 all-gather.10
  102.6 37.4 all-gather.12
  182.0 32.7 reduce-scatter.9
  252.2 63.4 reduce-scatter.7
  318.3 77.8 reduce-scatter.13
  398.8 77.9 reduce-scatter.11
  479.8 20.8 reduce-scatter.15
  505.0 233.3 all-reduce.5
where the time goes:
time: 761 us; the launch traced here: 752 us
  waiting for transfers between devices  440 us (58%)
  matrix products  127 us (17%)
  blocking collectives  90 us (12%)
  local copies, waits for them, and re-layouts  60.4 us (8%)
  other arithmetic  18.2 us (2%)
  between operations  15.8 us (2%)
    psum x1, waiting for transfers between devices, body(): lax.psum(lax.psum_scatter(grad_qkv, 'tensor', scatter_dimension=1, tiled=...  161 us
    reduce_scatter x1, waiting for transfers between devices, body(): lax.psum_scatter(grad_up, 'tensor', scatter_dimension=0, tiled=True)  80.6 us
    reduce_scatter x1, waiting for transfers between devices, body(): lax.psum_scatter(grad_down, 'tensor', scatter_dimension=0, tiled=True)  80.5 us
    psum x1, blocking collectives, body(): lax.psum((grad_out_bias, grad_gain_mid, grad_shift_mid, grad_down_bias, g...  45.4 us
    reduce_scatter x1, waiting for transfers between devices, body(): lax.psum_scatter(grad_qkv, 'tensor', scatter_dimension=1, tiled=True)  36 us
    all_gather x1, waiting for transfers between devices, body(): w_up = lax.all_gather(up_weight, 'tensor', axis=0, tiled=True)  34.8 us
    unnamed x83, local copies, waits for them, and re-layouts  28.7 us
    all_gather x1, waiting for transfers between devices, body(): w_down = lax.all_gather(down_weight, 'tensor', axis=0, tiled=True)  26 us
  transfers between devices with their start and end apart: 10, of which 8 were waited for; matrix products, arithmetic and copies ran while one was open for 20% of the time, Pallas kernels for 0%

commit v1 on v0

--- a/solution.py
+++ b/solution.py
@@ -163,7 +163,10 @@
     input_grad = (
         first_grad + jnp.einsum("crl,cld->rd", projected_grad, w_qkv, preferred_element_type=F32)
     ).astype(BF16)
-    grad_qkv = lax.psum(lax.psum_scatter(grad_qkv, "tensor", scatter_dimension=1, tiled=True), "dp")
+    grad_qkv = jnp.sum(
+        lax.all_gather(lax.psum_scatter(grad_qkv, "tensor", scatter_dimension=1, tiled=True), "dp"),
+        axis=0,
+    )
     grad_qv_bias = lax.psum(
         lax.psum_scatter(grad_qv_bias, "tensor", scatter_dimension=1, tiled=True), "dp"
     )

time: 761 us -> 938 us (1.23)
  waiting for transfers between devices: 440 us -> 614 us
    all_gather x0 -> x1, waiting for transfers between devices: none -> 124 us  [body(): lax.all_gather(lax.psum_scatter(grad_qkv, 'tensor', scatter_dimension=1,...]
    reduce_scatter x1, waiting for transfers between devices: 0.02 us -> 35.7 us  [body(): lax.psum_scatter(grad_out_weight, 'tensor', scatter_dimension=0, tiled=True)]
    psum x1, waiting for transfers between devices: 161 us -> 180 us  [body(): lax.psum(lax.psum_scatter(grad_out_weight, 'tensor', scatter_dimension=0,...]
    unnamed x83 -> x80, local copies, waits for them, and re-layouts: 28.7 us -> 27.8 us
  transfers between devices with their start and end apart: 10 -> 11, of which waited for: 8 -> 10; matrix products, arithmetic and copies ran while one was open for 20% -> 10% of each run, Pallas kernels for 0% -> 0%
where the time goes in v1:
time: 938 us; the launch traced here: 930 us
  waiting for transfers between devices  614 us (65%)
  matrix products  122 us (13%)
  blocking collectives  89.3 us (10%)
  local copies, waits for them, and re-layouts  62.2 us (7%)
  other arithmetic  25.6 us (3%)
  between operations  15.6 us (2%)
    psum x1, waiting for transfers between devices, body(): lax.psum(lax.psum_scatter(grad_out_weight, 'tensor', scatter_dimension=0,...  180 us
    all_gather x1, waiting for transfers between devices, body(): lax.all_gather(lax.psum_scatter(grad_qkv, 'tensor', scatter_dimension=1,...  124 us
    reduce_scatter x1, waiting for transfers between devices, body(): lax.psum_scatter(grad_down, 'tensor', scatter_dimension=0, tiled=True)  80.6 us
    reduce_scatter x1, waiting for transfers between devices, body(): lax.psum_scatter(grad_up, 'tensor', scatter_dimension=0, tiled=True)  80.6 us
    psum x1, blocking collectives, body(): lax.psum((grad_out_bias, grad_gain_mid, grad_shift_mid, grad_down_bias, g...  45.4 us
    reduce_scatter x1, waiting for transfers between devices, body(): lax.psum_scatter(grad_out_weight, 'tensor', scatter_dimension=0, tiled=True)  35.7 us
    all_gather x1, waiting for transfers between devices, body(): w_up = lax.all_gather(up_weight, 'tensor', axis=0, tiled=True)  34.8 us
    reduce_scatter x1, waiting for transfers between devices, body(): lax.psum_scatter(grad_qkv, 'tensor', scatter_dimension=1, tiled=True)  31.8 us
  transfers between devices with their start and end apart: 11, of which 10 were waited for; matrix products, arithmetic and copies ran while one was open for 10% of the time, Pallas kernels for 0%

profile of v1, /device:TPU:0, one launch (start us, length us, event | category | flops | bytes accessed | tf_op | source)
XLA Modules:
  0.0 929.5 jit_solution(15874388353317299020)
XLA Ops:
  10.3 6.0 all-gather.1
  17.2 1.6 copy.80
  18.9 5.5 all-gather.2
  24.4 1.6 copy.88
  26.2 16.9 %all-gather.9.cloned.1.call-done = bf16[3,768,768]{2,1,0:T(8,128)(2,1)} async-done(((bf16[3,192,768]{2,1,0:T(8,128)(2,1)}), bf16[3,768,768]{2,1,0:T(8,128)(2,1)}) %all-gather.9.cloned.1.call-update) | async-done | bytes 3538960 | tf_op jit(solution)/shard_map/all_gather | solution.py:63
  43.2 6.1 fusion.8
  49.3 1.1 slice_bitcast_fusion.1
  52.0 1.1 fusion.41
  53.1 2.7 fusion.64
  55.8 1.0 fusion.27
  56.7 1.6 copy-done.7
  58.4 2.4 copy.86
  60.8 1.4 all-gather.11.cloned.1.call-done
  62.2 3.8 fusion.65
  66.4 34.8 %all-gather.13.cloned.1.call-done = bf16[3072,768]{1,0:T(8,128)(2,1)} async-done(((bf16[768,768]{1,0:T(8,128)(2,1)}), bf16[3072,768]{1,0:T(8,128)(2,1)}) %all-gather.13.cloned.1.call-update) | async-done | bytes 4718608 | tf_op jit(solution)/shard_map/all_gather | solution.py:66
  101.2 13.0 %multiply_convert_fusion = (bf16[1024,3072]{1,0:T(8,128)(2,1)}, f32[1024,3072]{1,0:T(8,128)}) fusion(f32[3072]{0:T(1024)S(1)} %bitcast.119, bf16[3072,768]{1,0:T(8,128)(2,1)} %all-gather.13.cloned.1.call-done, f32[1024,768]{0,1:T(8,128)S(1)} %get-tuple-element.91, f32[768]{0:T(1024)S(1)} %convert_element_type.102, f32[768]{0:T(1024)S(1)} %convert_element_type.101, ...), kind=kOutput, calls=%fused_computation.9 | convolution fusion | flops 4854644736 | bytes 26765312 | tf_op jit(solution)/shard_map/rd,fd->rf/dot_general | solution.py:103
  114.2 25.9 %all-gather.15.cloned.1.call-done = bf16[3072,768]{1,0:T(8,128)(2,1)} async-done(((bf16[768,768]{1,0:T(8,128)(2,1)}), bf16[3072,768]{1,0:T(8,128)(2,1)}) %all-gather.15.cloned.1.call-update) | async-done | bytes 4718608 | tf_op jit(solution)/shard_map/all_gather | solution.py:68
  140.1 9.4 %fusion.66 = (f32[1024]{0:T(1024)S(1)}, f32[1024,768]{0,1:T(8,128)S(1)}) fusion(f32[768]{0:T(1024)S(1)} %convert_element_type.106, bf16[1024,3072]{1,0:T(8,128)(2,1)} %get-tuple-element.92, bf16[3072,768]{1,0:T(8,128)(2,1)} %all-gather.15.cloned.1.call-done, f32[768]{0:T(1024)S(1)} %convert_element_type.102, f32[768]{0:T(1024)S(1)} %convert_element_type.101, ...), kind=kOutput, calls=%fused_computation.113 | convolution fusion | flops 4837342208 | bytes 17323008 | tf_op jit(solution)/shard_map/dot_general | solution.py:106
  149.9 1.0 copy-done.4
  152.4 12.6 %convert_reduce_fusion = (f32[3072]{0:T(1024)S(1)}, bf16[1024,3072]{1,0:T(8,128)(2,1)}) fusion(f32[1024,3072]{1,0:T(8,128)} %get-tuple-element.93, f32[3072]{0:T(1024)S(1)} %bitcast.120, bf16[3072,768]{1,0:T(8,128)(2,1)S(1)} %copy-done.24, f32[1024]{0:T(1024)S(1)} %get-tuple-element.101, f32[1024,768]{0,1:T(8,128)S(1)} %get-tuple-element.95, ...), kind=kOutput, calls=%fused_computation.8 | convolution fusion | flops 4880593920 | bytes 28359680 | tf_op jit(solution)/shard_map/rd,fd->rf/dot_general | solution.py:120
  165.0 10.8 %multiply_reduce_fusion.2 = (f32[768]{0:T(1024)S(1)}, f32[1024]{0:T(1024)S(1)}, f32[1024]{0:T(1024)S(1)}, f32[768]{0:T(1024)S(1)}, f32[1024,768]{0,1:T(8,128)S(1)}) fusion(f32[1024,768]{0,1:T(8,128)S(1)} %copy-done.6, f32[1024]{0:T(1024)S(1)} %add_rsqrt_fusion.1, f32[1024]{0:T(1024)S(1)} %broadcast_multiply_fusion.5, f32[768]{0:T(1024)S(1)} %convert_element_type.101, ...), kind=kOutput, calls=%fused_computation.23 | convolution fusion | flops 4846776320 | bytes 22069248 | tf_op jit(solution)/shard_map/dot_general | solution.py:128
  175.9 1.1 fusion.61
  177.0 1.6 copy-done.8
  178.6 2.6 convolution_convert_fusion.1
  181.2 2.7 copy.90
  184.0 2.0 copy.124
  186.0 7.5 multiply_reduce_fusion
  193.6 5.0 multiply_convert_fusion.1
  198.5 1.0 fusion.25
  199.9 3.4 fusion.26
  203.3 3.4 fusion.30
  206.8 2.4 copy.95
  209.2 3.7 stack_reshape.12
  212.9 2.6 copy.102
  215.5 3.8 copy.98
  219.3 3.7 stack_reshape.13
  222.9 2.8 copy.103
  225.7 3.8 copy.101
  229.5 3.7 stack_reshape.14
  233.2 2.6 copy.104
  235.7 9.7 %fusion.20 = f32[3,768,768]{2,1,0:T(8,128)} fusion(bf16[1024,768]{1,0:T(8,128)(2,1)} %param.17, bf16[1,1024,768]{2,1,0:T(8,128)(2,1)} %copy.104, bf16[1,1024,768]{2,1,0:T(8,128)(2,1)} %copy.103, bf16[1,1024,768]{2,1,0:T(8,128)(2,1)} %copy.102), kind=kOutput, calls=%fused_computation.58 | convolution fusion | flops 3628597248 | bytes 13369344 | tf_op jit(solution)/shard_map/crl,rd->cld/dot_general | solution.py:160
  245.5 5.2 fusion.17
  250.8 10.9 %fusion.47 = f32[3072,768]{1,0:T(8,128)} fusion(bf16[1024,3072]{1,0:T(8,128)(2,1)} %get-tuple-element.92, bf16[1024,768]{0,1:T(8,128)(2,1)} %copy.88, f32[1024,768]{0,1:T(8,128)S(1)} %get-tuple-element.95, f32[1024]{0:T(1024)S(1)} %get-tuple-element.101, f32[1024]{0:T(1024)S(1)} %get-tuple-element.102, f32[1024]{0:T(1024)S(1)} %get-tuple-element.86, ...), kind=kOutput, calls=%fused_computation.81 | convolution fusion | flops 4839702528 | bytes 20470784 | tf_op jit(solution)/shard_map/rf,rd->fd/dot_general | solution.py:116
  261.8 11.2 %fusion.56 = f32[3072,768]{1,0:T(8,128)} fusion(bf16[1024,3072]{1,0:T(8,128)(2,1)} %get-tuple-element.100, f32[1024,768]{0,1:T(8,128)} %copy-done.5, f32[768]{0:T(1024)S(1)} %convert_element_type.102, f32[768]{0:T(1024)S(1)} %convert_element_type.101, f32[1024]{0:T(1024)S(1)} %add_rsqrt_fusion.1, f32[1024]{0:T(1024)S(1)} %broadcast_multiply_fusion.5), kind=kOutput, calls=%fused_computation.105 | convolution fusion | flops 4835770368 | bytes 18888704 | tf_op jit(solution)/shard_map/rf,rd->fd/dot_general | solution.py:122
  273.1 2.7 convert_reduce_fusion.1
  275.8 0.9 copy.118
  276.8 31.8 %reduce-scatter.8.cloned.1.call-done = f32[3,192,768]{2,1,0:T(8,128)} async-done(((f32[3,768,768]{2,1,0:T(8,128)}), f32[3,192,768]{2,1,0:T(8,128)}) %reduce-scatter.8.cloned.1.call-update) | async-done | bytes 1769488 | tf_op jit(solution)/shard_map/reduce_scatter | solution.py:167
  308.7 35.7 %reduce-scatter.10.cloned.1.call-done = f32[192,768]{1,0:T(8,128)} async-done(((f32[768,768]{1,0:T(8,128)}), f32[192,768]{1,0:T(8,128)}) %reduce-scatter.10.cloned.1.call-update) | async-done | bytes 589840 | tf_op jit(solution)/shard_map/reduce_scatter | solution.py:136
  344.5 80.6 %reduce-scatter.14.cloned.1.call-done = f32[768,768]{1,0:T(8,128)} async-done(((f32[3072,768]{1,0:T(8,128)}), f32[768,768]{1,0:T(8,128)}) %reduce-scatter.14.cloned.1.call-update) | async-done | bytes 2359312 | tf_op jit(solution)/shard_map/reduce_scatter | solution.py:118
  425.0 80.6 %reduce-scatter.12.cloned.1.call-done = f32[768,768]{1,0:T(8,128)} async-done(((f32[3072,768]{1,0:T(8,128)}), f32[768,768]{1,0:T(8,128)}) %reduce-scatter.12.cloned.1.call-update) | async-done | bytes 2359312 | tf_op jit(solution)/shard_map/reduce_scatter | solution.py:124
  506.9 9.4 %fusion.9 = bf16[1024,768]{0,1:T(8,128)(2,1)} fusion(f32[1024,768]{0,1:T(8,128)} %copy-done.8, bf16[3,768,768]{2,1,0:T(8,128)(2,1)} %all-gather.9.cloned.1.call-done, bf16[1,1024,768]{2,1,0:T(8,128)(2,1)} %copy.104, bf16[1,1024,768]{2,1,0:T(8,128)(2,1)} %copy.103, bf16[1,1024,768]{2,1,0:T(8,128)(2,1)} %copy.102), kind=kOutput, calls=%fused_computation.21 | convolution fusion | flops 3630170112 | bytes 12976128 | tf_op jit(solution)/shard_map/crl,cld->rd/dot_general | solution.py:164
  516.3 2.6 copy.108
  518.8 4.2 multiply_reduce_fusion.1
  523.1 2.6 copy.107
  525.7 10.1 %all-reduce = f32[3072]{0:T(1024)S(1)} all-reduce(f32[3072]{0:T(1024)S(1)} %get-tuple-element.99), channel_id=7, replica_groups=mesh['dp'=8,'tensor'=4] {'tensor'}, use_global_device_ids=true, to_apply=%region_27.28.clone | all-reduce | flops 3072 | bytes 24576
  535.9 45.4 %all-reduce.1 = (f32[768]{0:T(1024)}, f32[768]{0:T(1024)}, f32[768]{0:T(1024)}, f32[768]{0:T(1024)}, f32[768]{0:T(1024)}, /*index=5*/f32[768]{0:T(1024)}) all-reduce(f32[768]{0:T(1024)S(1)} %get-tuple-element.76, f32[768]{0:T(1024)S(1)} %get-tuple-element.56, ...), channel_id=1, replica_groups=mesh['dp'=8,'tensor'=4] {'dp','tensor'}, use_global_device_ids=true, to_apply=%region_19.20 | all-reduce | flops 4608 | bytes 36864 | tf_op jit(solution)/shard_map/psum | solution.py:174
  581.3 1.0 copy.119
  582.3 22.3 %all-reduce.2 = (f32[2,192]{1,0:T(2,128)}, f32[768]{0:T(1024)}) all-reduce(f32[2,192]{1,0:T(2,128)S(1)} %copy.119, f32[768]{0:T(1024)S(1)} %dynamic-slice.1), channel_id=1, replica_groups=mesh['dp'=8,'tensor'=4] {'dp'}, use_global_device_ids=true, to_apply=%region_15.16 | all-reduce | flops 1152 | bytes 9216 | tf_op jit(solution)/shard_map/psum | solution.py:170
  604.5 123.9 %all-gather.17.cloned.1.call-done = f32[24,192,768]{2,1,0:T(8,128)} async-done(((f32[3,192,768]{2,1,0:T(8,128)}), f32[24,192,768]{2,1,0:T(8,128)}) %all-gather.17.cloned.1.call-update) | async-done | bytes 14155792 | tf_op jit(solution)/shard_map/all_gather | solution.py:167
  728.5 7.3 reduce_sum.181
  735.8 180.0 %all-reduce.6.cloned.1.call-done = (f32[192,768]{1,0:T(8,128)}, f32[768,768]{1,0:T(8,128)}, f32[768,768]{1,0:T(8,128)}) async-done(((f32[192,768]{1,0:T(8,128)}, f32[768,768]{1,0:T(8,128)}, f32[768,768]{1,0:T(8,128)}), (f32[192,768]{1,0:T(8,128)}, f32[768,768]{1,0:T(8,128)}, f32[768,768]{1,0:T(8,128)})) %all-reduce.6.cloned.1.call-update) | async-done | bytes 5308432 | tf_op jit(solution)/shard_map/psum | solution.py:135
  915.8 2.1 copy.158
  917.9 3.2 copy.159
  921.1 1.4 copy.160
  (117 shorter events, 9.5 us)
Async XLA Ops:
  7.2 3.0 copy-start.26
  7.2 3.0 copy-start.27
  7.2 3.1 copy-start.23
  7.2 10.0 %copy-start.11 = (bf16[1024,768]{1,0:T(8,128)(2,1)S(1)}, bf16[1024,768]{1,0:T(8,128)(2,1)}, u32[]{:S(2)}) copy-start(bf16[1024,768]{1,0:T(8,128)(2,1)} %param.17) | copy-start | bytes 4718596
  7.2 35.9 %all-gather.9.cloned.1.call-start = ((), (), s32[]{:S(2)}) async-start(), calls=%async_computation.5 | async-start | bytes 4423680 | tf_op jit(solution)/shard_map/all_gather | solution.py:63
  8.0 10.9 %copy-start.16 = (bf16[768]{0:T(1024)(128)(2,1)S(1)}, bf16[768]{0:T(1024)(128)(2,1)}, u32[]{:S(2)}) copy-start(bf16[768]{0:T(1024)(128)(2,1)} %param.21) | copy-start | bytes 4612
  8.0 10.9 %copy-start.17 = (bf16[768]{0:T(1024)(128)(2,1)S(1)}, bf16[768]{0:T(1024)(128)(2,1)}, u32[]{:S(2)}) copy-start(bf16[768]{0:T(1024)(128)(2,1)} %param.22) | copy-start | bytes 4612
  8.0 10.9 %copy-start.18 = (bf16[768]{0:T(1024)(128)(2,1)S(1)}, bf16[768]{0:T(1024)(128)(2,1)}, u32[]{:S(2)}) copy-start(bf16[768]{0:T(1024)(128)(2,1)} %param.23) | copy-start | bytes 4612
  8.0 10.9 %copy-start.22 = (bf16[768]{0:T(1024)(128)(2,1)S(1)}, bf16[768]{0:T(1024)(128)(2,1)}, u32[]{:S(2)}) copy-start(bf16[768]{0:T(1024)(128)(2,1)} %param.25) | copy-start | bytes 4612
  8.0 16.4 %copy-start.19 = (bf16[768]{0:T(1024)(128)(2,1)S(1)}, bf16[768]{0:T(1024)(128)(2,1)}, u32[]{:S(2)}) copy-start(bf16[768]{0:T(1024)(128)(2,1)} %param.27) | copy-start | bytes 4612
  8.0 16.4 %copy-start.10 = (bf16[1024,768]{1,0:T(8,128)(2,1)S(1)}, bf16[1024,768]{1,0:T(8,128)(2,1)}, u32[]{:S(2)}) copy-start(bf16[1024,768]{1,0:T(8,128)(2,1)} %param.30) | copy-start | bytes 4718596
  8.0 54.2 %all-gather.11.cloned.1.call-start = ((), (), s32[]{:S(2)}) async-start(), calls=%async_computation.6 | async-start | bytes 1474560 | tf_op jit(solution)/shard_map/all_gather | solution.py:65
  8.8 92.4 %all-gather.13.cloned.1.call-start = ((), (), s32[]{:S(2)}) async-start(), calls=%async_computation.7 | async-start | bytes 5898240 | tf_op jit(solution)/shard_map/all_gather | solution.py:66
  9.5 130.6 %all-gather.15.cloned.1.call-start = ((), (), s32[]{:S(2)}) async-start(), calls=%async_computation.8 | async-start | bytes 5898240 | tf_op jit(solution)/shard_map/all_gather | solution.py:68
  10.1 298.6 %reduce-scatter.8.cloned.1.call-start = ((), (), s32[]{:S(2)}) async-start(), calls=%async_computation.9 | async-start | bytes 8847360 | tf_op jit(solution)/shard_map/reduce_scatter | solution.py:167
  17.2 8.9 copy-start.20
  50.8 1.2 copy-start
  51.3 1.8 copy-start.2
  51.7 4.0 copy-start.12
  55.8 2.6 copy-start.7
  66.0 48.2 %copy-start.5 = (f32[1024,768]{0,1:T(8,128)}, f32[1024,768]{0,1:T(8,128)S(1)}, u32[]{:S(2)}) copy-start(f32[1024,768]{0,1:T(8,128)S(1)} %get-tuple-element.91) | copy-start | bytes 9437188
  149.5 1.4 copy-start.4
  149.9 2.5 copy-start.24
  152.4 12.6 %copy-start.6 = (f32[1024,768]{0,1:T(8,128)S(1)}, f32[1024,768]{0,1:T(8,128)}, u32[]{:S(2)}) copy-start(f32[1024,768]{0,1:T(8,128)} %copy-done.5) | copy-start | bytes 9437188
  175.9 2.8 copy-start.25
  177.0 1.6 copy-start.8
  184.0 2.0 copy-start.13
  186.0 7.6 copy-start.14
  186.0 7.6 slice-start
  186.0 7.5 slice-start.1
  193.5 5.0 copy-start.3
  198.5 1.4 copy-start.1
  199.9 3.4 copy-start.15
  245.5 99.0 %reduce-scatter.10.cloned.1.call-start = ((), (), s32[]{:S(2)}) async-start(), calls=%async_computation.10 | async-start | bytes 2949120 | tf_op jit(solution)/shard_map/reduce_scatter | solution.py:136
  250.8 174.3 %reduce-scatter.14.cloned.1.call-start = ((), (), s32[]{:S(2)}) async-start(), calls=%async_computation.12 | async-start | bytes 11796480 | tf_op jit(solution)/shard_map/reduce_scatter | solution.py:118
  261.8 243.8 %reduce-scatter.12.cloned.1.call-start = ((), (), s32[]{:S(2)}) async-start(), calls=%async_computation.11 | async-start | bytes 11796480 | tf_op jit(solution)/shard_map/reduce_scatter | solution.py:124
  273.1 308.2 %reduce-scatter.16.cloned.1.call-start = ((), (), s32[]{:S(2)}) async-start(), calls=%async_computation.14 | async-start | bytes 491520
  276.8 451.7 %all-gather.17.cloned.1.call-start = ((), (), s32[]{:S(2)}) async-start(), calls=%async_computation.13 | async-start | bytes 15925248 | tf_op jit(solution)/shard_map/all_gather | solution.py:167
  308.7 197.0 %copy-start.21 = (bf16[768]{0:T(1024)(128)(2,1)S(1)}, bf16[768]{0:T(1024)(128)(2,1)}, u32[]{:S(2)}) copy-start(bf16[768]{0:T(1024)(128)(2,1)} %param.29) | copy-start | bytes 4612
  308.7 197.0 %copy-start.28 = (u32[32]{0:T(128)S(1)}, u32[32]{0:T(128)}, u32[]{:S(2)}) copy-start(u32[32]{0:T(128)} %constant.52) | copy-start | bytes 388
  308.7 607.1 %all-reduce.6.cloned.1.call-start = ((), (), s32[]{:S(2)}) async-start(), calls=%async_computation.15 | async-start | bytes 10616832 | tf_op jit(solution)/shard_map/psum | solution.py:135
  915.8 5.3 copy-start.9
Sparse Core Ops, SparseCore 0:
  9.6 33.5 all-gather.8
  44.7 17.4 all-gather.10
  63.7 37.4 all-gather.12
  102.6 37.4 all-gather.14
  245.6 63.0 reduce-scatter.7
  311.6 32.8 reduce-scatter.9
  347.1 77.9 reduce-scatter.13
  427.6 77.9 reduce-scatter.11
  508.7 20.8 reduce-scatter.15
  531.6 196.8 all-gather.16
  732.5 183.2 all-reduce.5
